TPU v7x, 32 devices: a whole 2x2x4 slice. The times are simulated.
32 devices in a mesh: parts: 2 (over y), row: 4 (over x, core), col: 4 (over z).
Axes of the slice: x: 2, y: 2, z: 4, core: 2. Of those that a mesh axis runs over, the one named last changes fastest.
Arguments:
- basis: float32 [2048, 16384], P(('parts', 'row'), 'col'), parts along dimension 0, may hold values from -6 to 6
- panel_one: float32 [32768, 256], P(('parts', 'col', 'row')), parts along dimension 0, may hold values from -192 to 192
- panel_two: float32 [32768, 256], P(('parts', 'col', 'row')), parts along dimension 0, may hold values from -192 to 192
- gradient: float32 [2048, 512], P(('parts', 'row')), parts along dimension 0, may hold values from -0.25 to 0.25
Outputs:
- new_basis: float32 [2048, 16384], P(('parts', 'row'), 'col'), parts along dimension 0
- rotated: float32 [1024, 16384], P(('parts', 'row'), 'col'), parts along dimension 0
There are 2 independent parts, one for each index of `parts`. A program takes and returns all parts, laid end to end along the dimension named above; each array names one. Nothing has to cross between parts.
All inputs are finite; a program needn't handle non-finite values.
Results may differ from a plain program's by a relative error of at most 0.0001.
Values sent between devices are 32-bit elements; how exact they have to be, the bound alone decides.
No kernel may reach another device: no remote copies, remote signals or barrier semaphores. Data moves between devices by JAX's collectives and lax.ppermute only.
A program may use at most 64 MiB of HBM per device.

v0:
```python
import jax
import jax.numpy as jnp
from jax import lax
from jax.sharding import PartitionSpec as P


def dot_high(left, right):
    return jnp.dot(left, right, precision=lax.Precision.HIGHEST, preferred_element_type=jnp.float32)


def inner_rows(left, right):
    return jnp.einsum(
        "ra,rb->ab",
        left,
        right,
        precision=lax.Precision.HIGHEST,
        preferred_element_type=jnp.float32,
    )


def outer_cols(left, right):
    return jnp.einsum(
        "rk,ck->rc",
        left,
        right,
        precision=lax.Precision.HIGHEST,
        preferred_element_type=jnp.float32,
    )


def tri_inverse(upper):
    size = upper.shape[0]
    width = 8
    count = size // width
    shaped = upper.reshape(count, width, count, width)
    selector = jnp.eye(count, dtype=upper.dtype)
    blocks = jnp.einsum("iajb,ij->iab", shaped, selector, precision=lax.Precision.HIGHEST)
    inverse = jnp.zeros_like(blocks)
    unit = jnp.eye(width, dtype=upper.dtype)
    for line in range(width - 1, -1, -1):
        known = jnp.einsum(
            "bj,bjc->bc", blocks[:, line, :], inverse, precision=lax.Precision.HIGHEST
        )
        value = (unit[line][None, :] - known) / blocks[:, line, line][:, None]
        inverse = inverse.at[:, line, :].set(value)
    span = width
    while count > 1:
        shaped = upper.reshape(count, span, count, span)
        pairs = count // 2
        lefts = jnp.arange(pairs) * 2
        pick = (
            (jnp.arange(count)[None, :, None] == lefts[:, None, None])
            & (jnp.arange(count)[None, None, :] == lefts[:, None, None] + 1)
        ).astype(upper.dtype)
        corner = jnp.einsum("iajb,pij->pab", shaped, pick, precision=lax.Precision.HIGHEST)
        first = inverse[0::2]
        second = inverse[1::2]
        top = -jnp.einsum(
            "pab,pbc->pac",
            jnp.einsum("pab,pbc->pac", first, corner, precision=lax.Precision.HIGHEST),
            second,
            precision=lax.Precision.HIGHEST,
        )
        upper_half = jnp.concatenate([first, top], axis=2)
        lower_half = jnp.concatenate([jnp.zeros_like(second), second], axis=2)
        inverse = jnp.concatenate([upper_half, lower_half], axis=1)
        count = pairs
        span = span * 2
    return inverse[0]


def tri_factor(gram):
    upper = jnp.triu(gram, 1) + jnp.diag(jnp.diag(gram)) * 0.5
    return tri_inverse(upper)


def swap(value, distance, size):
    return lax.ppermute(value, "row", [(i, i ^ distance) for i in range(size)])


def spread(size):
    steps = []
    distance = 1
    while distance < size:
        steps.append(distance)
        distance *= 2
    return steps


def slot_order(me, size):
    steps = spread(size)
    order = []
    for slot in range(size):
        mask = 0
        for level, distance in enumerate(steps):
            if not (slot >> (len(steps) - 1 - level)) & 1:
                mask ^= distance
        order.append(mask)
    return jnp.array(order) ^ me


def col_sum(value):
    size = lax.axis_size("col")
    for distance in spread(size):
        value = value + lax.ppermute(
            value, "col", [(i, i ^ distance) for i in range(size)]
        )
    return value


def scatter_rows(value, size):
    for distance in spread(size):
        count = value.shape[0] // 2
        value = value[count:] + swap(value[:count], distance, size)
    return value


def shards(basis, panel_one, panel_two, gradient):
    size = lax.axis_size("row")
    k = panel_one.shape[1]
    span = panel_one.shape[0]
    lanes = gradient.shape[1] // size
    me = lax.axis_index("row")
    own = jnp.concatenate([panel_one, panel_two], axis=1)
    held = {0: own}
    for distance in reversed(spread(size)):
        keys = sorted(held)
        got = swap(jnp.stack([held[key] for key in keys]), distance, size)
        for index, key in enumerate(keys):
            held[key ^ distance] = got[index]
    held = jnp.stack([held[key] for key in range(size)])

    gram_own = inner_rows(own, own)
    gram_chip = gram_own + swap(gram_own, 1, size)
    half = me % 2
    rows = gram_chip.shape[0] // 2
    mine = col_sum(lax.dynamic_slice_in_dim(gram_chip, half * rows, rows, axis=0))
    for distance in spread(size)[1:]:
        mine = mine + swap(mine, distance, size)
    halves = jnp.stack([mine, swap(mine, 1, size)])
    gram = jnp.take(halves, jnp.array([0, 1]) ^ half, axis=0).reshape(2 * rows, -1)

    order = slot_order(me, size)
    shuffled = jnp.take(gradient.reshape(-1, size, lanes), order, axis=1).reshape(gradient.shape)
    head = inner_rows(shuffled, basis)
    count = head.shape[0] // 2
    head = head[count:] + swap(head[:count], 1, size)
    head, _ = lax.optimization_barrier((head, held))
    for distance in spread(size)[1:]:
        count = head.shape[0] // 2
        head = head[count:] + swap(head[:count], distance, size)

    image = None
    for slot in range(size):
        cols = lax.dynamic_slice_in_dim(basis, (me ^ slot) * span, span, axis=1)
        part = dot_high(cols, held[slot])
        image = part if image is None else image + part
    image = col_sum(image)

    gathered = jnp.take(held, jnp.arange(size) ^ me, axis=0).reshape(size * span, -1)
    factor_one = tri_factor(gram[:k, :k])
    factor_two = tri_factor(gram[k:, k:])
    first = dot_high(image[:, :k], factor_one)
    image_two = image[:, k:] - dot_high(first, gram[:k, k:])
    second = dot_high(image_two, factor_two)
    weight = jnp.concatenate([first, second], axis=1)
    new_basis = basis - outer_cols(weight, gathered)
    tail = scatter_rows(inner_rows(shuffled, weight), size)
    rotated = head - outer_cols(tail, gathered)
    return (new_basis, rotated)


def solution(mesh):
    return jax.shard_map(
        shards,
        mesh=mesh,
        in_specs=(
            P(("parts", "row"), "col"),
            P(("parts", "col", "row"), None),
            P(("parts", "col", "row"), None),
            P(("parts", "row"), None),
        ),
        out_specs=(P(("parts", "row"), "col"), P(("parts", "row"), "col")),
        check_vma=False,
    )
```

profile of v0, /device:TPU:0, one launch (start us, length us, event | category | flops | bytes accessed | tf_op | source)
XLA Modules:
  0.0 273.8 jit_solution(1447025730722436226)
XLA Ops:
  3.5 4.5 %fusion.140 = f32[512,512]{1,0:T(8,128)} fusion(f32[1024,512]{1,0:T(8,128)S(1)} %constant_dynamic-update-slice_fusion.14), kind=kOutput, calls=%fused_computation.297 | convolution fusion | flops 3221225472 | bytes 3145728 | tf_op jit(solution)/shard_map/ra,rb->ab/dot_general | solution.py:12
  12.4 9.2 %fusion.145 = f32[512,4096]{1,0:T(8,128)S(1)} fusion(f32[256,512]{0,1:T(8,128)S(1)} %bitcast_select_fusion.2, f32[256,4096]{1,0:T(8,128)} %param.38), kind=kOutput, calls=%fused_computation.302 | convolution fusion | flops 6442450944 | bytes 13107200 | tf_op jit(solution)/shard_map/ra,rb->ab/dot_general | solution.py:12
  21.6 3.2 %copy-done.1 = f32[512,4096]{1,0:T(8,128)} copy-done((f32[512,4096]{1,0:T(8,128)}, f32[512,4096]{1,0:T(8,128)S(1)}, u32[]{:S(2)}) %copy-start.1) | copy-done | bytes 8388632
  34.0 12.4 %collective-permute-done.5 = f32[256,512]{1,0:T(8,128)S(1)} collective-permute-done((f32[256,512]{1,0:T(8,128)S(1)}, f32[256,512]{1,0:T(8,128)S(1)}, u32[]{:S(2)}, u32[]{:S(2)}) %collective-permute-start.5) | collective-permute-done | bytes 524320 | tf_op jit(solution)/shard_map/ppermute | solution.py:105
  46.6 2.7 collective-permute-start.6
  49.3 22.8 %collective-permute-done.6 = f32[256,512]{1,0:T(8,128)S(1)} collective-permute-done((f32[256,512]{1,0:T(8,128)S(1)}, f32[256,512]{1,0:T(8,128)S(1)}, u32[]{:S(2)}, u32[]{:S(2)}) %collective-permute-start.6) | collective-permute-done | bytes 524320 | tf_op jit(solution)/shard_map/ppermute | solution.py:105
  73.4 4.0 %fusion.18 = f32[256,512]{1,0:T(8,128)} fusion(f32[1024,512]{1,0:T(8,128)S(1)} %constant_dynamic-update-slice_fusion.14, f32[256,4096]{1,0:T(8,128)} %param.38, s32[]{:T(128)S(6)} %select_n.85), kind=kOutput, calls=%fused_computation.41 | convolution fusion | flops 1610612736 | bytes 3670020 | tf_op jit(solution)/shard_map/dot_general | solution.py:8
  77.4 7.8 %collective-permute-done.7 = f32[256,512]{1,0:T(8,128)} collective-permute-done((f32[256,512]{1,0:T(8,128)S(1)}, f32[256,512]{1,0:T(8,128)}, u32[]{:S(2)}, u32[]{:S(2)}) %collective-permute-start.7) | collective-permute-done | bytes 524320 | tf_op jit(solution)/shard_map/ppermute | solution.py:78
  87.8 4.0 %pad_maximum_fusion.1 = f32[2,1024,512]{2,1,0:T(8,128)} fusion(f32[1,1024,512]{2,1,0:T(8,128)} %collective-permute-done, f32[1,1024,512]{2,1,0:T(8,128)S(1)} %bitcast.310), kind=kLoop, calls=%fused_computation.9 | loop fusion | flops 1048576 | bytes 8388608 | tf_op jit(solution)/shard_map/stack | solution.py:128
  92.4 4.7 %fusion.2 = f32[256,512]{1,0:T(8,128)} fusion(f32[1,1024,512]{2,1,0:T(8,128)} %collective-permute-done, f32[256,4096]{1,0:T(8,128)} %param.38, s32[]{:T(128)S(6)} %select_n.87), kind=kOutput, calls=%fused_computation.12 | convolution fusion | flops 1610612736 | bytes 3670020 | tf_op jit(solution)/shard_map/dot_general | solution.py:8
  99.1 2.8 %gather_fusion = f32[2,256,512]{2,1,0:T(8,128)} fusion(f32[2,256,512]{2,1,0:T(8,128)} %pad_maximum_fusion.2, s32[1024]{0:T(1024)S(1)} %pad_clamp_fusion.2), kind=kCustom, calls=%fused_computation | custom fusion | bytes 2097160 | tf_op jit(solution)/shard_map/jit(_take)/gather | solution.py:141
  110.2 3.8 %reshape.906 = f32[32,8,32,8]{3,2,1,0:T(8,128)} reshape(f32[256,256]{1,0:T(8,128)S(1)} %get-tuple-element.200) | data formatting | bytes 524288 | tf_op jit(solution)/shard_map/reshape | solution.py:35
  114.0 3.7 %fusion.79 = f32[32,1,8,8]{3,1,2,0:T(1,128)S(1)} fusion(f32[32,8,32,8]{3,2,1,0:T(8,128)} %reshape.906, pred[32,32,1,1]{1,0,2,3:T(32,128)(4,1)S(1)} %fusion.85), kind=kOutput, calls=%fused_computation.127 | convolution fusion | flops 786432 | bytes 271360 | tf_op jit(solution)/shard_map/iajb,ij->iab/dot_general | solution.py:37
  117.8 3.6 %reshape.921 = f32[32,8,32,8]{3,2,1,0:T(8,128)} reshape(f32[256,256]{1,0:T(8,128)S(1)} %get-tuple-element.201) | data formatting | bytes 524288 | tf_op jit(solution)/shard_map/reshape | solution.py:35
  121.5 3.7 %fusion.77 = f32[32,1,8,8]{3,1,2,0:T(1,128)S(1)} fusion(f32[32,8,32,8]{3,2,1,0:T(8,128)} %reshape.921, pred[32,32,1,1]{1,0,2,3:T(32,128)(4,1)S(1)} %fusion.85), kind=kOutput, calls=%fused_computation.125 | convolution fusion | flops 786432 | bytes 271360 | tf_op jit(solution)/shard_map/iajb,ij->iab/dot_general | solution.py:37
  129.1 5.7 %convolution_bitcast_fusion.6 = f32[16,8,8]{0,2,1:T(8,128)S(1)} fusion(f32[32,8,32,8]{3,2,1,0:T(8,128)} %reshape.921, pred[16,32]{1,0:T(8,128)(4,1)S(1)} %iota_compare_fusion.12, pred[16,32]{0,1:T(8,128)(4,1)S(1)} %iota_compare_fusion.9), kind=kOutput, calls=%fused_computation.34 | convolution fusion | flops 12599296 | bytes 267264 | tf_op jit(solution)/shard_map/iajb,pij->pab/dot_general | solution.py:55
  140.9 5.7 %convolution_bitcast_fusion.7 = f32[16,8,8]{0,2,1:T(8,128)S(1)} fusion(f32[32,8,32,8]{3,2,1,0:T(8,128)} %reshape.906, pred[16,32]{1,0:T(8,128)(4,1)S(1)} %iota_compare_fusion.12, pred[16,32]{0,1:T(8,128)(4,1)S(1)} %iota_compare_fusion.9), kind=kOutput, calls=%fused_computation.35 | convolution fusion | flops 12599296 | bytes 267264 | tf_op jit(solution)/shard_map/iajb,pij->pab/dot_general | solution.py:55
  155.2 2.7 convolution_bitcast_fusion.3
  166.9 2.7 %convolution_bitcast_fusion.5 = f32[8,16,16]{2,0,1:T(8,128)S(1)} fusion(f32[16,16,16,16]{3,2,1,0:T(8,128)} %reshape.915, pred[8,16]{1,0:T(8,128)(4,1)S(1)} %copy-done.14, pred[8,16]{0,1:T(8,128)(4,1)S(1)} %iota_compare_fusion.11), kind=kOutput, calls=%fused_computation.25 | convolution fusion | flops 6293504 | bytes 270592 | tf_op jit(solution)/shard_map/iajb,pij->pab/dot_general | solution.py:55
  176.8 3.8 %fusion = f32[256,512]{1,0:T(8,128)S(1)} fusion(f32[256,4096]{1,0:T(8,128)} %param.38, s32[]{:T(128)S(6)} %select_n.88, f32[2,1024,512]{2,1,0:T(8,128)} %collective-permute-done.1), kind=kOutput, calls=%fused_computation.10 | convolution fusion | flops 1610612736 | bytes 3670020 | tf_op jit(solution)/shard_map/dot_general | solution.py:8
  180.7 4.2 %fusion.12 = f32[256,512]{1,0:T(8,128)S(1)} fusion(f32[256,512]{1,0:T(8,128)S(1)} %fusion, f32[256,512]{1,0:T(8,128)} %fusion.2, f32[256,512]{1,0:T(8,128)} %fusion.18, f32[256,4096]{1,0:T(8,128)} %param.38, s32[]{:T(128)S(6)} %select_n.86, f32[2,1024,512]{2,1,0:T(8,128)} %collective-permute-done.1), kind=kOutput, calls=%fused_computation.19 | convolution fusion | flops 1611005952 | bytes 5242884 | tf_op jit(solution)/shard_map/dot_general | solution.py:8
  186.6 4.1 %slice_add_fusion = f32[256,4096]{1,0:T(8,128)S(1)} fusion(f32[256,4096]{1,0:T(8,128)} %collective-permute-done.9, f32[512,4096]{1,0:T(8,128)} %copy-done.1), kind=kLoop, calls=%fused_computation.8 | loop fusion | flops 1048576 | bytes 12582912 | tf_op jit(solution)/shard_map/add | solution.py:147
  190.7 8.0 %collective-permute-done.2 = f32[256,512]{1,0:T(8,128)S(1)} collective-permute-done((f32[256,512]{1,0:T(8,128)S(1)}, f32[256,512]{1,0:T(8,128)S(1)}, u32[]{:S(2)}, u32[]{:S(2)}) %collective-permute-start.2) | collective-permute-done | bytes 524320 | tf_op jit(solution)/shard_map/ppermute | solution.py:105
  198.8 3.4 %collective-permute-start.3 = (f32[256,512]{1,0:T(8,128)S(1)}, f32[256,512]{1,0:T(8,128)}, u32[]{:S(2)}, u32[]{:S(2)}) collective-permute-start(f32[256,512]{1,0:T(8,128)S(1)} %add.202), channel_id=1, source_target_pairs={{0,2},{1,3},{2,0},{3,1},{4,6},{5,7},{6,4},{7,5},{8,10},{9,11},{10,... | collective-permute-start | bytes 1572872 | tf_op jit(solution)/shard_map/ppermute | solution.py:105
  202.2 2.7 fusion.132
  204.9 5.1 %pad_maximum_fusion = f32[4,1024,512]{2,1,0:T(8,128)} fusion(f32[1,1024,512]{2,1,0:T(8,128)S(1)} %get-tuple-element.199, f32[1,1024,512]{2,1,0:T(8,128)} %collective-permute-done, f32[1,1024,512]{2,1,0:T(8,128)S(1)} %get-tuple-element.198, f32[1,1024,512]{2,1,0:T(8,128)S(1)} %bitcast.311), kind=kLoop, calls=%fused_computation.5 | loop fusion | flops 6291456 | bytes 16777216 | tf_op jit(solution)/shard_map/stack | solution.py:131
  210.8 7.8 %gather_fusion.3 = f32[4,1024,512]{2,1,0:T(8,128)} fusion(f32[4,1024,512]{2,1,0:T(8,128)} %pad_maximum_fusion, s32[1024]{0:T(1024)} %pad_clamp_fusion.1), kind=kCustom, calls=%fused_computation.3 | custom fusion | bytes 16777232 | tf_op jit(solution)/shard_map/jit(_take)/gather | solution.py:160
  218.6 6.5 %collective-permute-done.3 = f32[256,512]{1,0:T(8,128)} collective-permute-done((f32[256,512]{1,0:T(8,128)S(1)}, f32[256,512]{1,0:T(8,128)}, u32[]{:S(2)}, u32[]{:S(2)}) %collective-permute-start.3) | collective-permute-done | bytes 524320 | tf_op jit(solution)/shard_map/ppermute | solution.py:105
  230.0 4.0 %bitcast_select_fusion = f32[4096,512]{1,0:T(8,128)S(1)} fusion(f32[4,1024,512]{2,1,0:T(8,128)} %gather_fusion.3, pred[4096]{0:T(1024)(128)(4,1)S(1)} %bitcast.323), kind=kLoop, calls=%fused_computation.6 | loop fusion | flops 2097152 | bytes 16781312 | tf_op jit(solution)/shard_map/jit(_take)/select_n | solution.py:160
  234.8 15.5 %convolution_subtract_fusion = f32[256,4096]{1,0:T(8,128)} fusion(f32[256,4096]{1,0:T(8,128)S(1)} %copy-done, f32[4096,512]{1,0:T(8,128)S(1)} %bitcast_select_fusion, f32[256,256]{0,1:T(8,128)S(1)} %fusion.23, f32[256,256]{0,1:T(8,128)S(1)} %fusion.29), kind=kOutput, calls=%fused_computation.7 | convolution fusion | flops 6443630592 | bytes 17301504 | tf_op jit(solution)/shard_map/rk,ck->rc/dot_general | solution.py:22
  250.3 12.3 %collective-permute-done.12 = f32[128,512]{1,0:T(8,128)S(1)} collective-permute-done((f32[128,512]{1,0:T(8,128)S(1)}, f32[128,512]{1,0:T(8,128)S(1)}, u32[]{:S(2)}, u32[]{:S(2)}) %collective-permute-start.12) | collective-permute-done | bytes 262176 | tf_op jit(solution)/shard_map/ppermute | solution.py:78
  262.6 11.0 %add_subtract_fusion = f32[128,4096]{1,0:T(8,128)} fusion(f32[128,4096]{1,0:T(8,128)} %collective-permute-done.10, f32[256,4096]{1,0:T(8,128)S(1)} %copy-done.3, f32[4096,512]{1,0:T(8,128)S(1)} %bitcast_select_fusion, f32[128,512]{1,0:T(8,128)S(1)} %collective-permute-done.12, f32[256,512]{1,0:T(8,128)S(1)} %slice_add_fusion.1), kind=kOutput, calls=%fused_computation.16 | convolution fusion | flops 3222339584 | bytes 15204352 | tf_op jit(solution)/shard_map/rk,ck->rc/dot_general | solution.py:22
  (217 shorter events, 73.9 us)
Async XLA Ops:
  2.0 8.9 %copy-start.16 = (s32[4]{0:T(128)S(1)}, s32[4]{0:T(128)}, u32[]{:S(2)}) copy-start(s32[4]{0:T(128)} %constant.481.clone) | copy-start | bytes 52
  2.0 8.9 %copy-start.6 = (f32[256,512]{1,0:T(8,128)S(1)}, f32[256,512]{1,0:T(8,128)}, u32[]{:S(2)}) copy-start(f32[256,512]{1,0:T(8,128)} %param.41) | copy-start | bytes 1572868
  8.0 23.0 %collective-permute-start.4 = (f32[512,512]{1,0:T(8,128)}, f32[512,512]{1,0:T(8,128)}, u32[]{:S(2)}, u32[]{:S(2)}) collective-permute-start(f32[512,512]{1,0:T(8,128)} %fusion.140), channel_id=1, source_target_pairs={{0,4},{4,0},{8,12},{12,8},{1,5},{5,1},{9,13},{13,9},{2,6},{6,2},{1... | collective-permute-start | bytes 3145736 | tf_op jit(solution)/shard_map/ppermute | solution.py:78
  8.5 79.4 %collective-permute-start = (f32[1,1024,512]{2,1,0:T(8,128)S(1)}, f32[1,1024,512]{2,1,0:T(8,128)}, u32[]{:S(2)}, u32[]{:S(2)}) collective-permute-start(f32[1,1024,512]{2,1,0:T(8,128)S(1)} %bitcast.309), channel_id=1, source_target_pairs={{0,8},{4,12},{8,0},{12,4},{1,9},{5,13},{9,1},{13,5},{2,10},{6,14},... | collective-permute-start | bytes 6291464 | tf_op jit(solution)/shard_map/ppermute | solution.py:78
  21.6 3.2 %copy-start.1 = (f32[512,4096]{1,0:T(8,128)}, f32[512,4096]{1,0:T(8,128)S(1)}, u32[]{:S(2)}) copy-start(f32[512,4096]{1,0:T(8,128)S(1)} %fusion.145) | copy-start | bytes 25165828
  27.0 159.6 %collective-permute-start.9 = (f32[256,4096]{1,0:T(8,128)}, f32[256,4096]{1,0:T(8,128)}, u32[]{:S(2)}, u32[]{:S(2)}) collective-permute-start(f32[256,4096]{1,0:T(8,128)} %slice.700), channel_id=1, source_target_pairs={{0,4},{4,0},{8,12},{12,8},{1,5},{5,1},{9,13},{13,9},{2,6},{6,2},{1... | collective-permute-start | bytes 12582920 | tf_op jit(solution)/shard_map/ppermute | solution.py:78
  32.3 14.2 %collective-permute-start.5 = (f32[256,512]{1,0:T(8,128)S(1)}, f32[256,512]{1,0:T(8,128)S(1)}, u32[]{:S(2)}, u32[]{:S(2)}) collective-permute-start(f32[256,512]{1,0:T(8,128)S(1)} %dynamic-slice_add_fusion), channel_id=1, source_target_pairs={{0,1},{1,0},{2,3},{3,2},{4,5},{5,4},{6,7},{7,6},{8,9},{9,8},{10,11... | collective-permute-start | bytes 1572872 | tf_op jit(solution)/shard_map/ppermute | solution.py:105
  46.6 25.6 %collective-permute-start.6 = (f32[256,512]{1,0:T(8,128)S(1)}, f32[256,512]{1,0:T(8,128)S(1)}, u32[]{:S(2)}, u32[]{:S(2)}) collective-permute-start(f32[256,512]{1,0:T(8,128)S(1)} %add.208), channel_id=1, source_target_pairs={{0,2},{1,3},{2,0},{3,1},{4,6},{5,7},{6,4},{7,5},{8,10},{9,11},{10,... | collective-permute-start | bytes 1572872 | tf_op jit(solution)/shard_map/ppermute | solution.py:105
  72.2 13.0 %collective-permute-start.7 = (f32[256,512]{1,0:T(8,128)S(1)}, f32[256,512]{1,0:T(8,128)}, u32[]{:S(2)}, u32[]{:S(2)}) collective-permute-start(f32[256,512]{1,0:T(8,128)S(1)} %add.209), channel_id=1, source_target_pairs={{0,8},{4,12},{8,0},{12,4},{1,9},{5,13},{9,1},{13,5},{2,10},{6,14},... | collective-permute-start | bytes 1572872 | tf_op jit(solution)/shard_map/ppermute | solution.py:78
  87.1 9.9 %collective-permute-start.8 = (f32[256,512]{1,0:T(8,128)}, f32[256,512]{1,0:T(8,128)S(1)}, u32[]{:S(2)}, u32[]{:S(2)}) collective-permute-start(f32[256,512]{1,0:T(8,128)} %add.210), channel_id=1, source_target_pairs={{0,4},{4,0},{8,12},{12,8},{1,5},{5,1},{9,13},{13,9},{2,6},{6,2},{1... | collective-permute-start | bytes 1572872 | tf_op jit(solution)/shard_map/ppermute | solution.py:78
  91.9 84.9 %collective-permute-start.1 = (f32[2,1024,512]{2,1,0:T(8,128)}, f32[2,1024,512]{2,1,0:T(8,128)}, u32[]{:S(2)}, u32[]{:S(2)}) collective-permute-start(f32[2,1024,512]{2,1,0:T(8,128)} %pad_maximum_fusion.1), channel_id=1, source_target_pairs={{0,4},{4,0},{8,12},{12,8},{1,5},{5,1},{9,13},{13,9},{2,6},{6,2},{1... | collective-permute-start | bytes 12582920 | tf_op jit(solution)/shard_map/ppermute | solution.py:78
  103.3 1.0 copy-start.4
  146.6 8.4 %copy-start.8 = (f32[8,16,16]{0,2,1:T(8,128)S(1)}, f32[8,16,16]{0,2,1:T(8,128)}, u32[]{:S(2)}) copy-start(f32[8,16,16]{0,2,1:T(8,128)} %slice.630) | copy-start | bytes 24580
  146.6 8.5 %copy-start.7 = (f32[8,16,16]{0,2,1:T(8,128)S(1)}, f32[8,16,16]{0,2,1:T(8,128)}, u32[]{:S(2)}) copy-start(f32[8,16,16]{0,2,1:T(8,128)} %slice.631) | copy-start | bytes 24580
  146.6 8.6 %copy-start.14 = (pred[8,16]{1,0:T(8,128)(4,1)S(1)}, pred[8,16]{1,0:T(8,128)(4,1)}, u32[]{:S(2)}) copy-start(pred[8,16]{1,0:T(8,128)(4,1)} %iota_compare_fusion.14) | copy-start | bytes 388
  149.0 9.4 %copy-start.13 = (pred[4,8]{0,1:T(8,128)(4,1)S(1)}, pred[4,8]{0,1:T(8,128)(4,1)}, u32[]{:S(2)}) copy-start(pred[4,8]{0,1:T(8,128)(4,1)} %iota_compare_fusion.13) | copy-start | bytes 100
  151.8 9.0 %copy-start.15 = (pred[2,4]{0,1:T(4,128)(4,1)S(1)}, pred[2,4]{0,1:T(4,128)(4,1)}, u32[]{:S(2)}) copy-start(pred[2,4]{0,1:T(4,128)(4,1)} %iota_compare_fusion.16) | copy-start | bytes 28
  160.7 11.8 %copy-start.5 = (f32[4,64,4,64]{3,2,1,0:T(4,128)S(1)}, f32[4,64,4,64]{3,2,1,0:T(4,128)}, u32[]{:S(2)}) copy-start(f32[4,64,4,64]{3,2,1,0:T(4,128)} %reshape.917) | copy-start | bytes 786436
  166.9 7.4 %copy-start.9 = (f32[2,128,2,128]{3,2,1,0:T(2,128)S(1)}, f32[2,128,2,128]{3,2,1,0:T(2,128)}, u32[]{:S(2)}) copy-start(f32[2,128,2,128]{3,2,1,0:T(2,128)} %reshape.919) | copy-start | bytes 786436
  184.8 13.9 %collective-permute-start.2 = (f32[256,512]{1,0:T(8,128)S(1)}, f32[256,512]{1,0:T(8,128)S(1)}, u32[]{:S(2)}, u32[]{:S(2)}) collective-permute-start(f32[256,512]{1,0:T(8,128)S(1)} %fusion.12), channel_id=1, source_target_pairs={{0,1},{1,0},{2,3},{3,2},{4,5},{5,4},{6,7},{7,6},{8,9},{9,8},{10,11... | collective-permute-start | bytes 1572872 | tf_op jit(solution)/shard_map/ppermute | solution.py:105
  190.7 19.3 %copy-start.2 = (f32[256,4096]{1,0:T(8,128)}, f32[256,4096]{1,0:T(8,128)S(1)}, u32[]{:S(2)}) copy-start(f32[256,4096]{1,0:T(8,128)S(1)} %slice_add_fusion) | copy-start | bytes 12582916
  198.8 26.3 %collective-permute-start.3 = (f32[256,512]{1,0:T(8,128)S(1)}, f32[256,512]{1,0:T(8,128)}, u32[]{:S(2)}, u32[]{:S(2)}) collective-permute-start(f32[256,512]{1,0:T(8,128)S(1)} %add.202), channel_id=1, source_target_pairs={{0,2},{1,3},{2,0},{3,1},{4,6},{5,7},{6,4},{7,5},{8,10},{9,11},{10,... | collective-permute-start | bytes 1572872 | tf_op jit(solution)/shard_map/ppermute | solution.py:105
  210.1 18.2 %copy-start.10 = (f32[128,128]{1,0:T(8,128)S(1)}, f32[128,128]{1,0:T(8,128)}, u32[]{:S(2)}) copy-start(f32[128,128]{1,0:T(8,128)} %copy.184) | copy-start | bytes 196612
  210.2 18.2 %copy-start.11 = (f32[1,128,128]{2,1,0:T(8,128)S(1)}, f32[1,128,128]{2,1,0:T(8,128)}, u32[]{:S(2)}) copy-start(f32[1,128,128]{2,1,0:T(8,128)} %get-tuple-element.205) | copy-start | bytes 196612
  210.2 52.4 %collective-permute-start.10 = (f32[128,4096]{1,0:T(8,128)S(1)}, f32[128,4096]{1,0:T(8,128)}, u32[]{:S(2)}, u32[]{:S(2)}) collective-permute-start(f32[128,4096]{1,0:T(8,128)S(1)} %slice.641), channel_id=1, source_target_pairs={{0,8},{4,12},{8,0},{12,4},{1,9},{5,13},{9,1},{13,5},{2,10},{6,14},... | collective-permute-start | bytes 6291464 | tf_op jit(solution)/shard_map/ppermute | solution.py:78
  218.6 11.4 %copy-start.12 = (pred[1,8,4,128]{3,1,2,0:T(8,128)(4,1)S(1)}, pred[1,8,4,128]{3,1,2,0:T(8,128)(4,1)}, u32[]{:S(2)}) copy-start(pred[1,8,4,128]{3,1,2,0:T(8,128)(4,1)} %copy.308) | copy-start | bytes 12292
  229.9 4.1 %collective-permute-start.11 = (f32[256,512]{1,0:T(8,128)S(1)}, f32[256,512]{1,0:T(8,128)S(1)}, u32[]{:S(2)}, u32[]{:S(2)}) collective-permute-start(f32[256,512]{1,0:T(8,128)S(1)} %slice.702), channel_id=1, source_target_pairs={{0,4},{4,0},{8,12},{12,8},{1,5},{5,1},{9,13},{13,9},{2,6},{6,2},{1... | collective-permute-start | bytes 1572872 | tf_op jit(solution)/shard_map/ppermute | solution.py:78
  230.0 4.8 %copy-start = (f32[256,4096]{1,0:T(8,128)S(1)}, f32[256,4096]{1,0:T(8,128)}, u32[]{:S(2)}) copy-start(f32[256,4096]{1,0:T(8,128)} %param.38) | copy-start | bytes 12582916
  234.2 28.4 %copy-start.3 = (f32[256,4096]{1,0:T(8,128)S(1)}, f32[256,4096]{1,0:T(8,128)}, u32[]{:S(2)}) copy-start(f32[256,4096]{1,0:T(8,128)} %copy-done.2) | copy-start | bytes 12582916
  234.2 28.4 %collective-permute-start.12 = (f32[128,512]{1,0:T(8,128)S(1)}, f32[128,512]{1,0:T(8,128)S(1)}, u32[]{:S(2)}, u32[]{:S(2)}) collective-permute-start(f32[128,512]{1,0:T(8,128)S(1)} %slice.704), channel_id=1, source_target_pairs={{0,8},{4,12},{8,0},{12,4},{1,9},{5,13},{9,1},{13,5},{2,10},{6,14},... | collective-permute-start | bytes 786440 | tf_op jit(solution)/shard_map/ppermute | solution.py:78
where the time goes:
time: 278 us; the launch traced here: 274 us
  matrix products  98.3 us (35%)
  waiting for transfers between devices  69.9 us (25%)
  local copies, waits for them, and re-layouts  56 us (20%)
  other arithmetic  32.7 us (12%)
  starting transfers between devices  15 us (5%)
    ppermute x4, waiting for transfers between devices, col_sum(): lax.ppermute(value, 'col', [(i, i ^ distance) for i in range(size)])  49.8 us
    dot_general x2, matrix products, outer_cols(): jnp.einsum('rk,ck->rc', left, right, precision=lax.Precision.HIGHEST, pre...  26.5 us
    dot_general x8, matrix products, tri_inverse(): jnp.einsum('iajb,pij->pab', shaped, pick, precision=lax.Precision.HIGHEST)  23.5 us
    ppermute x9, waiting for transfers between devices, swap(): return lax.ppermute(value, 'row', [(i, i ^ distance) for i in range(size)])  20.1 us
    dot_general x7, matrix products, dot_high(): jnp.dot(left, right, precision=lax.Precision.HIGHEST, preferred_element_t...  19.2 us
    dot_general x3, matrix products, inner_rows(): jnp.einsum('ra,rb->ab', left, right, precision=lax.Precision.HIGHEST, pre...  14.7 us
    reshape x8, local copies, waits for them, and re-layouts, tri_inverse(): shaped = upper.reshape(count, span, count, span)  10.3 us
    ppermute x4, starting transfers between devices, col_sum(): lax.ppermute(value, 'col', [(i, i ^ distance) for i in range(size)])  9.46 us
  transfers between devices with their start and end apart: 13, of which 6 were waited for; matrix products, arithmetic and copies ran while one was open for 60% of the time, Pallas kernels for 0%

commit v1 on v0

--- a/solution.py
+++ b/solution.py
@@ -74,6 +74,73 @@
     return tri_inverse(upper)
 
 
+def tri_inverse_pair(uppers):
+    size = uppers[0].shape[0]
+    width = 8
+    count = size // width
+    selector = jnp.eye(count, dtype=uppers[0].dtype)
+    blocks = jnp.concatenate(
+        [
+            jnp.einsum(
+                "iajb,ij->iab",
+                upper.reshape(count, width, count, width),
+                selector,
+                precision=lax.Precision.HIGHEST,
+            )
+            for upper in uppers
+        ],
+        axis=0,
+    )
+    inverse = jnp.zeros_like(blocks)
+    unit = jnp.eye(width, dtype=blocks.dtype)
+    for line in range(width - 1, -1, -1):
+        known = jnp.einsum(
+            "bj,bjc->bc", blocks[:, line, :], inverse, precision=lax.Precision.HIGHEST
+        )
+        value = (unit[line][None, :] - known) / blocks[:, line, line][:, None]
+        inverse = inverse.at[:, line, :].set(value)
+    span = width
+    while count > 1:
+        pairs = count // 2
+        lefts = jnp.arange(pairs) * 2
+        pick = (
+            (jnp.arange(count)[None, :, None] == lefts[:, None, None])
+            & (jnp.arange(count)[None, None, :] == lefts[:, None, None] + 1)
+        ).astype(blocks.dtype)
+        corner = jnp.concatenate(
+            [
+                jnp.einsum(
+                    "iajb,pij->pab",
+                    upper.reshape(count, span, count, span),
+                    pick,
+                    precision=lax.Precision.HIGHEST,
+                )
+                for upper in uppers
+            ],
+            axis=0,
+        )
+        first = inverse[0::2]
+        second = inverse[1::2]
+        top = -jnp.einsum(
+            "pab,pbc->pac",
+            jnp.einsum("pab,pbc->pac", first, corner, precision=lax.Precision.HIGHEST),
+            second,
+            precision=lax.Precision.HIGHEST,
+        )
+        upper_half = jnp.concatenate([first, top], axis=2)
+        lower_half = jnp.concatenate([jnp.zeros_like(second), second], axis=2)
+        inverse = jnp.concatenate([upper_half, lower_half], axis=1)
+        count = pairs
+        span = span * 2
+    return inverse[0], inverse[1]
+
+
+def tri_factor_pair(grams):
+    return tri_inverse_pair(
+        [jnp.triu(gram, 1) + jnp.diag(jnp.diag(gram)) * 0.5 for gram in grams]
+    )
+
+
 def swap(value, distance, size):
     return lax.ppermute(value, "row", [(i, i ^ distance) for i in range(size)])
 
@@ -158,8 +225,7 @@
     image = col_sum(image)
 
     gathered = jnp.take(held, jnp.arange(size) ^ me, axis=0).reshape(size * span, -1)
-    factor_one = tri_factor(gram[:k, :k])
-    factor_two = tri_factor(gram[k:, k:])
+    factor_one, factor_two = tri_factor_pair([gram[:k, :k], gram[k:, k:]])
     first = dot_high(image[:, :k], factor_one)
     image_two = image[:, k:] - dot_high(first, gram[:k, k:])
     second = dot_high(image_two, factor_two)

time: 278 us -> 307 us (1.10)
  other arithmetic: 32.7 us -> 48.7 us
  local copies, waits for them, and re-layouts: 56 us -> 63.5 us
  matrix products: 98.3 us -> 103 us
    div x0 -> x9, other arithmetic: none -> 10.8 us  [tri_inverse_pair(): value = (unit[line][None, :] - known) / blocks[:, line, line][:, None]]
    concatenate x9 -> x10, other arithmetic: 0.62 us -> 8.19 us  [the longest x4 4.72 us: tri_inverse_pair(): jnp.concatenate([jnp.einsum('iajb,pij->pab', upper.reshape(count, span, c...]
    dot_general x30 -> x28, matrix products: 35.1 us -> 42.2 us  [the longest x8 24.9 us: tri_inverse_pair(): jnp.einsum('iajb,pij->pab', upper.reshape(count, span, count, span), pick...]
    squeeze x2 -> x8, local copies, waits for them, and re-layouts: 0.01 us -> 7.02 us  [tri_inverse_pair(): blocks[:, line, :]]
    scatter x0 -> x8, local copies, waits for them, and re-layouts: none -> 6.35 us  [tri_inverse_pair(): inverse = inverse.at[:, line, :].set(value)]
    slice x23 -> x6, local copies, waits for them, and re-layouts: 7.17 us -> 1.55 us  [the longest x5 1.51 us: tri_inverse_pair(): first = inverse[0::2]]
    unnamed x40 -> x36, local copies, waits for them, and re-layouts: 6.65 us -> 5.96 us
  transfers between devices with their start and end apart: 13 -> 13, of which waited for: 6 -> 6; matrix products, arithmetic and copies ran while one was open for 60% -> 65% of each run, Pallas kernels for 0% -> 0%
where the time goes in v1:
time: 307 us; the launch traced here: 301 us
  matrix products  103 us (34%)
  waiting for transfers between devices  68.8 us (22%)
  local copies, waits for them, and re-layouts  63.5 us (21%)
  other arithmetic  48.7 us (16%)
  starting transfers between devices  15.5 us (5%)
    ppermute x4, waiting for transfers between devices, col_sum(): lax.ppermute(value, 'col', [(i, i ^ distance) for i in range(size)])  47.8 us
    dot_general x2, matrix products, outer_cols(): jnp.einsum('rk,ck->rc', left, right, precision=lax.Precision.HIGHEST, pre...  26.8 us
    dot_general x8, matrix products, tri_inverse_pair(): jnp.einsum('iajb,pij->pab', upper.reshape(count, span, count, span), pick...  24.9 us
    ppermute x9, waiting for transfers between devices, swap(): return lax.ppermute(value, 'row', [(i, i ^ distance) for i in range(size)])  21 us
    dot_general x7, matrix products, dot_high(): jnp.dot(left, right, precision=lax.Precision.HIGHEST, preferred_element_t...  18.5 us
    dot_general x3, matrix products, inner_rows(): jnp.einsum('ra,rb->ab', left, right, precision=lax.Precision.HIGHEST, pre...  14.4 us
    div x9, other arithmetic, tri_inverse_pair(): value = (unit[line][None, :] - known) / blocks[:, line, line][:, None]  10.8 us
    dot_general x8, matrix products, tri_inverse_pair(): jnp.einsum('bj,bjc->bc', blocks[:, line, :], inverse, precision=lax.Preci...  9.61 us
  transfers between devices with their start and end apart: 13, of which 6 were waited for; matrix products, arithmetic and copies ran while one was open for 65% of the time, Pallas kernels for 0%

profile of v1, /device:TPU:0, one launch (start us, length us, event | category | flops | bytes accessed | tf_op | source)
XLA Modules:
  0.0 301.0 jit_solution(17436305983159481154)
XLA Ops:
  3.5 3.0 %collective-permute-start = (f32[1,1024,512]{2,1,0:T(8,128)S(1)}, f32[1,1024,512]{2,1,0:T(8,128)}, u32[]{:S(2)}, u32[]{:S(2)}) collective-permute-start(f32[1,1024,512]{2,1,0:T(8,128)S(1)} %bitcast.265), channel_id=1, source_target_pairs={{0,8},{4,12},{8,0},{12,4},{1,9},{5,13},{9,1},{13,5},{2,10},{6,14},... | collective-permute-start | bytes 6291464 | tf_op jit(solution)/shard_map/ppermute | solution.py:145
  6.5 4.5 %fusion.146 = f32[512,512]{1,0:T(8,128)} fusion(f32[1024,512]{1,0:T(8,128)S(1)} %constant_dynamic-update-slice_fusion), kind=kOutput, calls=%fused_computation.276 | convolution fusion | flops 3221225472 | bytes 3145728 | tf_op jit(solution)/shard_map/ra,rb->ab/dot_general | solution.py:12
  12.4 8.9 %fusion.153 = f32[512,4096]{1,0:T(8,128)S(1)} fusion(f32[256,512]{0,1:T(8,128)S(1)} %bitcast_select_fusion.2, f32[256,4096]{1,0:T(8,128)} %param.22), kind=kOutput, calls=%fused_computation.283 | convolution fusion | flops 6442450944 | bytes 13107200 | tf_op jit(solution)/shard_map/ra,rb->ab/dot_general | solution.py:12
  21.3 3.3 %copy-done.4 = f32[512,4096]{1,0:T(8,128)} copy-done((f32[512,4096]{1,0:T(8,128)}, f32[512,4096]{1,0:T(8,128)S(1)}, u32[]{:S(2)}) %copy-start.4) | copy-done | bytes 8388632
  31.9 12.2 %collective-permute-done.5 = f32[256,512]{1,0:T(8,128)S(1)} collective-permute-done((f32[256,512]{1,0:T(8,128)S(1)}, f32[256,512]{1,0:T(8,128)S(1)}, u32[]{:S(2)}, u32[]{:S(2)}) %collective-permute-start.5) | collective-permute-done | bytes 524320 | tf_op jit(solution)/shard_map/ppermute | solution.py:172
  44.2 2.7 collective-permute-start.6
  46.9 22.5 %collective-permute-done.6 = f32[256,512]{1,0:T(8,128)S(1)} collective-permute-done((f32[256,512]{1,0:T(8,128)S(1)}, f32[256,512]{1,0:T(8,128)S(1)}, u32[]{:S(2)}, u32[]{:S(2)}) %collective-permute-start.6) | collective-permute-done | bytes 524320 | tf_op jit(solution)/shard_map/ppermute | solution.py:172
  71.5 4.0 %fusion.18 = f32[256,512]{1,0:T(8,128)} fusion(f32[1024,512]{1,0:T(8,128)S(1)} %constant_dynamic-update-slice_fusion, f32[256,4096]{1,0:T(8,128)} %param.22, s32[]{:T(128)S(6)} %select_n.85), kind=kOutput, calls=%fused_computation.38 | convolution fusion | flops 1610612736 | bytes 3670020 | tf_op jit(solution)/shard_map/dot_general | solution.py:8
  75.4 7.1 %collective-permute-done.7 = f32[256,512]{1,0:T(8,128)} collective-permute-done((f32[256,512]{1,0:T(8,128)S(1)}, f32[256,512]{1,0:T(8,128)}, u32[]{:S(2)}, u32[]{:S(2)}) %collective-permute-start.7) | collective-permute-done | bytes 524320 | tf_op jit(solution)/shard_map/ppermute | solution.py:145
  84.6 4.0 %pad_maximum_fusion.1 = f32[2,1024,512]{2,1,0:T(8,128)} fusion(f32[1,1024,512]{2,1,0:T(8,128)} %collective-permute-done, f32[1,1024,512]{2,1,0:T(8,128)S(1)} %bitcast.266), kind=kLoop, calls=%fused_computation.9 | loop fusion | flops 1048576 | bytes 8388608 | tf_op jit(solution)/shard_map/stack | solution.py:195
  89.1 4.7 %fusion.2 = f32[256,512]{1,0:T(8,128)} fusion(f32[1,1024,512]{2,1,0:T(8,128)} %collective-permute-done, f32[256,4096]{1,0:T(8,128)} %param.22, s32[]{:T(128)S(6)} %select_n.87), kind=kOutput, calls=%fused_computation.12 | convolution fusion | flops 1610612736 | bytes 3670020 | tf_op jit(solution)/shard_map/dot_general | solution.py:8
  95.9 2.9 gather_fusion
  113.6 4.1 %reshape.640 = f32[32,8,32,8]{3,2,1,0:T(8,128)} reshape(f32[256,256]{1,0:T(8,128)S(1)} %get-tuple-element.104) | data formatting | bytes 524288 | tf_op jit(solution)/shard_map/reshape | solution.py:86
  117.7 3.7 %reshape.639 = f32[32,8,32,8]{3,2,1,0:T(8,128)} reshape(f32[256,256]{1,0:T(8,128)S(1)} %get-tuple-element.105) | data formatting | bytes 524288 | tf_op jit(solution)/shard_map/reshape | solution.py:86
  121.4 5.8 %convolution_bitcast_fusion.6 = f32[16,8,8]{0,2,1:T(8,128)S(1)} fusion(f32[32,8,32,8]{3,2,1,0:T(8,128)} %reshape.640, pred[16,32]{1,0:T(8,128)(4,1)S(1)} %iota_compare_fusion.10, pred[16,32]{0,1:T(8,128)(4,1)S(1)} %iota_compare_fusion.7), kind=kOutput, calls=%fused_computation.31 | convolution fusion | flops 12599296 | bytes 267264 | tf_op jit(solution)/shard_map/iajb,pij->pab/dot_general | solution.py:112
  127.2 3.5 %convolution_bitcast_fusion.7 = f32[16,8,8]{0,2,1:T(8,128)S(1)} fusion(f32[32,8,32,8]{3,2,1,0:T(8,128)S(1)} %copy-done.1, pred[16,32]{1,0:T(8,128)(4,1)S(1)} %iota_compare_fusion.10, pred[16,32]{0,1:T(8,128)(4,1)S(1)} %iota_compare_fusion.7), kind=kOutput, calls=%fused_computation.32 | convolution fusion | flops 12599296 | bytes 267264 | tf_op jit(solution)/shard_map/iajb,pij->pab/dot_general | solution.py:112
  139.8 2.5 convolution_bitcast_fusion.2
  181.3 3.3 %convolution_bitcast_fusion.4 = f32[8,16,16]{2,0,1:T(8,128)} fusion(f32[16,16,16,16]{3,2,1,0:T(8,128)} %reshape.650, pred[8,16]{1,0:T(8,128)(4,1)} %iota_compare_fusion.12, pred[8,16]{0,1:T(8,128)(4,1)S(1)} %iota_compare_fusion.9), kind=kOutput, calls=%fused_computation.29 | convolution fusion | flops 6293504 | bytes 270592 | tf_op jit(solution)/shard_map/iajb,pij->pab/dot_general | solution.py:112
  189.3 2.7 convolution_bitcast_fusion.5
  202.9 3.5 %fusion = f32[256,512]{1,0:T(8,128)S(1)} fusion(f32[256,4096]{1,0:T(8,128)S(1)} %copy-done.2, s32[]{:T(128)S(6)} %select_n.88, f32[2,1024,512]{2,1,0:T(8,128)} %collective-permute-done.1), kind=kOutput, calls=%fused_computation.10 | convolution fusion | flops 1610612736 | bytes 3670020 | tf_op jit(solution)/shard_map/dot_general | solution.py:8
  206.4 3.6 %fusion.12 = f32[256,512]{1,0:T(8,128)S(1)} fusion(f32[256,512]{1,0:T(8,128)S(1)} %fusion, f32[256,512]{1,0:T(8,128)S(1)} %copy-done.10, f32[256,512]{1,0:T(8,128)S(1)} %copy-done.9, f32[256,4096]{1,0:T(8,128)S(1)} %copy-done.2, s32[]{:T(128)S(6)} %select_n.86, f32[2,1024,512]{2,1,0:T(8,128)} %collective-permute-done.1), kind=kOutput, calls=%fused_computation.19 | convolution fusion | flops 1611005952 | bytes 5242884 | tf_op jit(solution)/shard_map/dot_general | solution.py:8
  211.8 3.9 %slice_add_fusion = f32[256,4096]{1,0:T(8,128)S(1)} fusion(f32[256,4096]{1,0:T(8,128)} %collective-permute-done.9, f32[512,4096]{1,0:T(8,128)} %copy-done.4), kind=kLoop, calls=%fused_computation.8 | loop fusion | flops 1048576 | bytes 12582912 | tf_op jit(solution)/shard_map/add | solution.py:214
  215.7 8.2 %collective-permute-done.2 = f32[256,512]{1,0:T(8,128)S(1)} collective-permute-done((f32[256,512]{1,0:T(8,128)S(1)}, f32[256,512]{1,0:T(8,128)S(1)}, u32[]{:S(2)}, u32[]{:S(2)}) %collective-permute-start.2) | collective-permute-done | bytes 524320 | tf_op jit(solution)/shard_map/ppermute | solution.py:172
  224.0 3.4 %collective-permute-start.3 = (f32[256,512]{1,0:T(8,128)S(1)}, f32[256,512]{1,0:T(8,128)}, u32[]{:S(2)}, u32[]{:S(2)}) collective-permute-start(f32[256,512]{1,0:T(8,128)S(1)} %add.170), channel_id=1, source_target_pairs={{0,2},{1,3},{2,0},{3,1},{4,6},{5,7},{6,4},{7,5},{8,10},{9,11},{10,... | collective-permute-start | bytes 1572872 | tf_op jit(solution)/shard_map/ppermute | solution.py:172
  227.4 2.7 fusion.139
  230.1 5.4 %pad_maximum_fusion = f32[4,1024,512]{2,1,0:T(8,128)} fusion(f32[1,1024,512]{2,1,0:T(8,128)S(1)} %get-tuple-element.103, f32[1,1024,512]{2,1,0:T(8,128)} %collective-permute-done, f32[1,1024,512]{2,1,0:T(8,128)S(1)} %get-tuple-element.102, f32[1,1024,512]{2,1,0:T(8,128)S(1)} %bitcast.267), kind=kLoop, calls=%fused_computation.5 | loop fusion | flops 6291456 | bytes 16777216 | tf_op jit(solution)/shard_map/stack | solution.py:198
  237.5 7.9 %gather_fusion.3 = f32[4,1024,512]{2,1,0:T(8,128)} fusion(f32[4,1024,512]{2,1,0:T(8,128)} %pad_maximum_fusion, s32[1024]{0:T(1024)} %pad_clamp_fusion.1), kind=kCustom, calls=%fused_computation.3 | custom fusion | bytes 16777232 | tf_op jit(solution)/shard_map/jit(_take)/gather | solution.py:227
  245.3 4.9 %collective-permute-done.3 = f32[256,512]{1,0:T(8,128)} collective-permute-done((f32[256,512]{1,0:T(8,128)S(1)}, f32[256,512]{1,0:T(8,128)}, u32[]{:S(2)}, u32[]{:S(2)}) %collective-permute-start.3) | collective-permute-done | bytes 524320 | tf_op jit(solution)/shard_map/ppermute | solution.py:172
  255.4 4.0 %bitcast_select_fusion = f32[4096,512]{1,0:T(8,128)S(1)} fusion(f32[4,1024,512]{2,1,0:T(8,128)} %gather_fusion.3, pred[4096]{0:T(1024)(128)(4,1)S(1)} %bitcast.294), kind=kLoop, calls=%fused_computation.6 | loop fusion | flops 2097152 | bytes 16781312 | tf_op jit(solution)/shard_map/jit(_take)/select_n | solution.py:227
  260.1 15.5 %convolution_subtract_fusion = f32[256,4096]{1,0:T(8,128)} fusion(f32[256,4096]{1,0:T(8,128)S(1)} %copy-done.3, f32[4096,512]{1,0:T(8,128)S(1)} %bitcast_select_fusion, f32[256,256]{0,1:T(8,128)S(1)} %fusion.22, f32[256,256]{0,1:T(8,128)S(1)} %fusion.25), kind=kOutput, calls=%fused_computation.7 | convolution fusion | flops 6443630592 | bytes 17301504 | tf_op jit(solution)/shard_map/rk,ck->rc/dot_general | solution.py:22
  275.6 13.9 %collective-permute-done.12 = f32[128,512]{1,0:T(8,128)S(1)} collective-permute-done((f32[128,512]{1,0:T(8,128)S(1)}, f32[128,512]{1,0:T(8,128)S(1)}, u32[]{:S(2)}, u32[]{:S(2)}) %collective-permute-start.12) | collective-permute-done | bytes 262176 | tf_op jit(solution)/shard_map/ppermute | solution.py:145
  289.5 11.3 %add_subtract_fusion = f32[128,4096]{1,0:T(8,128)} fusion(f32[128,4096]{1,0:T(8,128)} %collective-permute-done.10, f32[256,4096]{1,0:T(8,128)S(1)} %copy-done.6, f32[4096,512]{1,0:T(8,128)S(1)} %bitcast_select_fusion, f32[128,512]{1,0:T(8,128)S(1)} %collective-permute-done.12, f32[256,512]{1,0:T(8,128)S(1)} %slice_add_fusion.1), kind=kOutput, calls=%fused_computation.16 | convolution fusion | flops 3222339584 | bytes 15204352 | tf_op jit(solution)/shard_map/rk,ck->rc/dot_general | solution.py:22
  (186 shorter events, 105.9 us)
Async XLA Ops:
  2.0 9.0 %copy-start.14 = (s32[4]{0:T(128)S(1)}, s32[4]{0:T(128)}, u32[]{:S(2)}) copy-start(s32[4]{0:T(128)} %constant.322.clone) | copy-start | bytes 52
  2.0 9.0 %copy-start.12 = (f32[256,512]{1,0:T(8,128)S(1)}, f32[256,512]{1,0:T(8,128)}, u32[]{:S(2)}) copy-start(f32[256,512]{1,0:T(8,128)} %param.25) | copy-start | bytes 1572868
  3.5 81.1 %collective-permute-start = (f32[1,1024,512]{2,1,0:T(8,128)S(1)}, f32[1,1024,512]{2,1,0:T(8,128)}, u32[]{:S(2)}, u32[]{:S(2)}) collective-permute-start(f32[1,1024,512]{2,1,0:T(8,128)S(1)} %bitcast.265), channel_id=1, source_target_pairs={{0,8},{4,12},{8,0},{12,4},{1,9},{5,13},{9,1},{13,5},{2,10},{6,14},... | collective-permute-start | bytes 6291464 | tf_op jit(solution)/shard_map/ppermute | solution.py:145
  11.0 17.9 %collective-permute-start.4 = (f32[512,512]{1,0:T(8,128)}, f32[512,512]{1,0:T(8,128)}, u32[]{:S(2)}, u32[]{:S(2)}) collective-permute-start(f32[512,512]{1,0:T(8,128)} %fusion.146), channel_id=1, source_target_pairs={{0,4},{4,0},{8,12},{12,8},{1,5},{5,1},{9,13},{13,9},{2,6},{6,2},{1... | collective-permute-start | bytes 3145736 | tf_op jit(solution)/shard_map/ppermute | solution.py:145
  21.3 3.3 %copy-start.4 = (f32[512,4096]{1,0:T(8,128)}, f32[512,4096]{1,0:T(8,128)S(1)}, u32[]{:S(2)}) copy-start(f32[512,4096]{1,0:T(8,128)S(1)} %fusion.153) | copy-start | bytes 25165828
  26.9 184.9 %collective-permute-start.9 = (f32[256,4096]{1,0:T(8,128)}, f32[256,4096]{1,0:T(8,128)}, u32[]{:S(2)}, u32[]{:S(2)}) collective-permute-start(f32[256,4096]{1,0:T(8,128)} %slice.413), channel_id=1, source_target_pairs={{0,4},{4,0},{8,12},{12,8},{1,5},{5,1},{9,13},{13,9},{2,6},{6,2},{1... | collective-permute-start | bytes 12582920 | tf_op jit(solution)/shard_map/ppermute | solution.py:145
  30.2 13.9 %collective-permute-start.5 = (f32[256,512]{1,0:T(8,128)S(1)}, f32[256,512]{1,0:T(8,128)S(1)}, u32[]{:S(2)}, u32[]{:S(2)}) collective-permute-start(f32[256,512]{1,0:T(8,128)S(1)} %dynamic-slice_add_fusion), channel_id=1, source_target_pairs={{0,1},{1,0},{2,3},{3,2},{4,5},{5,4},{6,7},{7,6},{8,9},{9,8},{10,11... | collective-permute-start | bytes 1572872 | tf_op jit(solution)/shard_map/ppermute | solution.py:172
  44.2 25.3 %collective-permute-start.6 = (f32[256,512]{1,0:T(8,128)S(1)}, f32[256,512]{1,0:T(8,128)S(1)}, u32[]{:S(2)}, u32[]{:S(2)}) collective-permute-start(f32[256,512]{1,0:T(8,128)S(1)} %add.176), channel_id=1, source_target_pairs={{0,2},{1,3},{2,0},{3,1},{4,6},{5,7},{6,4},{7,5},{8,10},{9,11},{10,... | collective-permute-start | bytes 1572872 | tf_op jit(solution)/shard_map/ppermute | solution.py:172
  69.5 13.0 %collective-permute-start.7 = (f32[256,512]{1,0:T(8,128)S(1)}, f32[256,512]{1,0:T(8,128)}, u32[]{:S(2)}, u32[]{:S(2)}) collective-permute-start(f32[256,512]{1,0:T(8,128)S(1)} %add.177), channel_id=1, source_target_pairs={{0,8},{4,12},{8,0},{12,4},{1,9},{5,13},{9,1},{13,5},{2,10},{6,14},... | collective-permute-start | bytes 1572872 | tf_op jit(solution)/shard_map/ppermute | solution.py:145
  84.4 9.3 %collective-permute-start.8 = (f32[256,512]{1,0:T(8,128)}, f32[256,512]{1,0:T(8,128)S(1)}, u32[]{:S(2)}, u32[]{:S(2)}) collective-permute-start(f32[256,512]{1,0:T(8,128)} %add.178), channel_id=1, source_target_pairs={{0,4},{4,0},{8,12},{12,8},{1,5},{5,1},{9,13},{13,9},{2,6},{6,2},{1... | collective-permute-start | bytes 1572872 | tf_op jit(solution)/shard_map/ppermute | solution.py:145
  88.6 114.2 %collective-permute-start.1 = (f32[2,1024,512]{2,1,0:T(8,128)}, f32[2,1024,512]{2,1,0:T(8,128)}, u32[]{:S(2)}, u32[]{:S(2)}) collective-permute-start(f32[2,1024,512]{2,1,0:T(8,128)} %pad_maximum_fusion.1), channel_id=1, source_target_pairs={{0,4},{4,0},{8,12},{12,8},{1,5},{5,1},{9,13},{13,9},{2,6},{6,2},{1... | collective-permute-start | bytes 12582920 | tf_op jit(solution)/shard_map/ppermute | solution.py:145
  100.1 1.0 copy-start.7
  121.4 5.8 %copy-start.1 = (f32[32,8,32,8]{3,2,1,0:T(8,128)S(1)}, f32[32,8,32,8]{3,2,1,0:T(8,128)}, u32[]{:S(2)}) copy-start(f32[32,8,32,8]{3,2,1,0:T(8,128)} %reshape.639) | copy-start | bytes 786436
  127.2 5.0 %copy-start = (f32[32,8,32,8]{3,2,1,0:T(8,128)S(1)}, f32[32,8,32,8]{3,2,1,0:T(8,128)}, u32[]{:S(2)}) copy-start(f32[32,8,32,8]{3,2,1,0:T(8,128)} %reshape.640) | copy-start | bytes 786436
  189.2 10.4 %copy-start.11 = (f32[4,64,64]{2,0,1:T(4,128)S(1)}, f32[4,64,64]{2,0,1:T(4,128)}, u32[]{:S(2)}) copy-start(f32[4,64,64]{2,0,1:T(4,128)} %pad_maximum_fusion.8) | copy-start | bytes 196612
  189.3 11.0 %copy-start.15 = (pred[2,2,1]{1,0,2:T(4,128)(4,1)S(1)}, pred[2,2,1]{1,0,2:T(4,128)(4,1)}, u32[]{:S(2)}) copy-start(pred[2,2,1]{1,0,2:T(4,128)(4,1)} %and_bitcast_fusion) | copy-start | bytes 16
  195.2 5.1 %copy-start.13 = (f32[2,128,2,128]{3,2,1,0:T(2,128)S(1)}, f32[2,128,2,128]{3,2,1,0:T(2,128)}, u32[]{:S(2)}) copy-start(f32[2,128,2,128]{3,2,1,0:T(2,128)} %reshape.656) | copy-start | bytes 786436
  196.5 6.4 %copy-start.2 = (f32[256,4096]{1,0:T(8,128)S(1)}, f32[256,4096]{1,0:T(8,128)}, u32[]{:S(2)}) copy-start(f32[256,4096]{1,0:T(8,128)} %param.22) | copy-start | bytes 12582916
  199.6 6.8 %copy-start.9 = (f32[256,512]{1,0:T(8,128)S(1)}, f32[256,512]{1,0:T(8,128)}, u32[]{:S(2)}) copy-start(f32[256,512]{1,0:T(8,128)} %fusion.18) | copy-start | bytes 1572868
  199.6 6.8 %copy-start.10 = (f32[256,512]{1,0:T(8,128)S(1)}, f32[256,512]{1,0:T(8,128)}, u32[]{:S(2)}) copy-start(f32[256,512]{1,0:T(8,128)} %fusion.2) | copy-start | bytes 1572868
  210.0 13.9 %collective-permute-start.2 = (f32[256,512]{1,0:T(8,128)S(1)}, f32[256,512]{1,0:T(8,128)S(1)}, u32[]{:S(2)}, u32[]{:S(2)}) collective-permute-start(f32[256,512]{1,0:T(8,128)S(1)} %fusion.12), channel_id=1, source_target_pairs={{0,1},{1,0},{2,3},{3,2},{4,5},{5,4},{6,7},{7,6},{8,9},{9,8},{10,11... | collective-permute-start | bytes 1572872 | tf_op jit(solution)/shard_map/ppermute | solution.py:172
  215.7 19.7 %copy-start.5 = (f32[256,4096]{1,0:T(8,128)}, f32[256,4096]{1,0:T(8,128)S(1)}, u32[]{:S(2)}) copy-start(f32[256,4096]{1,0:T(8,128)S(1)} %slice_add_fusion) | copy-start | bytes 12582916
  224.0 26.3 %collective-permute-start.3 = (f32[256,512]{1,0:T(8,128)S(1)}, f32[256,512]{1,0:T(8,128)}, u32[]{:S(2)}, u32[]{:S(2)}) collective-permute-start(f32[256,512]{1,0:T(8,128)S(1)} %add.170), channel_id=1, source_target_pairs={{0,2},{1,3},{2,0},{3,1},{4,6},{5,7},{6,4},{7,5},{8,10},{9,11},{10,... | collective-permute-start | bytes 1572872 | tf_op jit(solution)/shard_map/ppermute | solution.py:172
  236.9 14.5 %copy-start.8 = (f32[2,256,256]{2,1,0:T(8,128)S(1)}, f32[2,256,256]{2,1,0:T(8,128)}, u32[]{:S(2)}) copy-start(f32[2,256,256]{2,1,0:T(8,128)} %select_maximum_fusion) | copy-start | bytes 1572868
  236.9 52.5 %collective-permute-start.10 = (f32[128,4096]{1,0:T(8,128)}, f32[128,4096]{1,0:T(8,128)}, u32[]{:S(2)}, u32[]{:S(2)}) collective-permute-start(f32[128,4096]{1,0:T(8,128)} %slice.358), channel_id=1, source_target_pairs={{0,8},{4,12},{8,0},{12,4},{1,9},{5,13},{9,1},{13,5},{2,10},{6,14},... | collective-permute-start | bytes 6291464 | tf_op jit(solution)/shard_map/ppermute | solution.py:145
  255.3 4.1 %collective-permute-start.11 = (f32[256,512]{1,0:T(8,128)S(1)}, f32[256,512]{1,0:T(8,128)S(1)}, u32[]{:S(2)}, u32[]{:S(2)}) collective-permute-start(f32[256,512]{1,0:T(8,128)S(1)} %slice.415), channel_id=1, source_target_pairs={{0,4},{4,0},{8,12},{12,8},{1,5},{5,1},{9,13},{13,9},{2,6},{6,2},{1... | collective-permute-start | bytes 1572872 | tf_op jit(solution)/shard_map/ppermute | solution.py:145
  255.4 4.8 %copy-start.3 = (f32[256,4096]{1,0:T(8,128)S(1)}, f32[256,4096]{1,0:T(8,128)}, u32[]{:S(2)}) copy-start(f32[256,4096]{1,0:T(8,128)} %param.22) | copy-start | bytes 12582916
  259.5 29.9 %copy-start.6 = (f32[256,4096]{1,0:T(8,128)S(1)}, f32[256,4096]{1,0:T(8,128)}, u32[]{:S(2)}) copy-start(f32[256,4096]{1,0:T(8,128)} %copy-done.5) | copy-start | bytes 12582916
  259.5 29.9 %collective-permute-start.12 = (f32[128,512]{1,0:T(8,128)S(1)}, f32[128,512]{1,0:T(8,128)S(1)}, u32[]{:S(2)}, u32[]{:S(2)}) collective-permute-start(f32[128,512]{1,0:T(8,128)S(1)} %slice.417), channel_id=1, source_target_pairs={{0,8},{4,12},{8,0},{12,4},{1,9},{5,13},{9,1},{13,5},{2,10},{6,14},... | collective-permute-start | bytes 786440 | tf_op jit(solution)/shard_map/ppermute | solution.py:145
